TPU v7x, 512 devices: a whole 4x4x16 slice. The times are simulated.
512 devices in a mesh: seq: 64 (over z, y), tensor: 8 (over x, core).
Axes of the slice: x: 4, y: 4, z: 16, core: 2. Of those that a mesh axis runs over, the one named last changes fastest.
Arguments:
- hidden: bfloat16 [8192, 4096], P('seq', 'tensor')
- norm_gain: bfloat16 [4096], replicated, may hold values from 0.5 to 1.5
- w_query: bfloat16 [4096, 4096], P('seq', 'tensor')
- key_value_weight: bfloat16 [4096, 1024], P('seq')
- w_out: bfloat16 [4096, 4096], P('tensor', 'seq'), may hold values from -0.09375 to 0.09375
- prefix_key_cache: bfloat16 [64, 1024, 1024], P('seq')
- prefix_owner: int32 [64], replicated, may hold values from 0 to 63, each once
- token_counts: int32 [64, 64], P('seq'), may hold values from 0 to 4, as said below
Outputs:
- attn_out: bfloat16 [8192, 4096], P('seq', 'tensor')
- suffix_key_cache: bfloat16 [8192, 1024], P('seq', 'tensor')
Inputs may be any that keep to these rules, and one draw needn't show every extreme that they name: `token_counts`: each row sums to 128; one prefix receives exactly 4 tokens from every sequence index.
All inputs are finite; a program needn't handle non-finite values.
Results may differ from a plain program's by a relative error of at most 0.035.
Values may be sent and summed in bfloat16 or wider, within the bound.
No kernel may reach another device: no remote copies, remote signals or barrier semaphores. Data moves between devices by JAX's collectives and lax.ppermute only.
A program may use at most 64 MiB of HBM per device.

v0:
```python
import jax
import jax.numpy as jnp
from jax import lax
from jax.sharding import PartitionSpec as P

HEAD_DIM = 128
PREFIX_LENGTH = 1024
eps = 1e-06
theta = 5000000.0


def rotate(values, positions):
    half = values.shape[-1] // 2
    frequency = theta ** (-jnp.arange(half, dtype=jnp.float32) * 2.0 / values.shape[-1])
    angle = positions.astype(jnp.float32)[:, None] * frequency[None, :]
    cosine = jnp.cos(angle)[:, None, :]
    sine = jnp.sin(angle)[:, None, :]
    first = values[..., :half]
    second = values[..., half:]
    return jnp.concatenate(
        [first * cosine - second * sine, second * cosine + first * sine], axis=-1
    )


def layout(counts_row, length):
    ends = jnp.cumsum(counts_row)
    starts = ends - counts_row
    places = jnp.arange(length, dtype=jnp.int32)
    member = (places[:, None] >= starts[None, :]) & (places[:, None] < ends[None, :])
    labels = jnp.arange(counts_row.shape[0], dtype=jnp.int32)
    prefix_group = jnp.sum(jnp.where(member, labels[None, :], 0), axis=1)
    offset = places - jnp.sum(jnp.where(member, starts[None, :], 0), axis=1)
    return (starts, prefix_group, offset)


def attend(query_vectors, keys, values, allowed):
    scores = lax.dot_general(
        query_vectors, keys, (((1,), (1,)), ((), ())), preferred_element_type=jnp.float32
    )
    scores = scores * (1.0 / query_vectors.shape[-1] ** 0.5)
    if allowed is not None:
        scores = jnp.where(allowed, scores, -1e30)
    top = jnp.max(scores, axis=1, keepdims=True)
    expo = jnp.exp(scores - top)
    total = jnp.sum(expo, axis=1, keepdims=True)
    weights = (expo / total).astype(jnp.bfloat16)
    result = jnp.dot(weights, values, preferred_element_type=jnp.float32)
    return (result, top[:, 0] + jnp.log(total[:, 0]))


def shards(
    hidden,
    norm_gain,
    w_query,
    key_value_weight,
    w_out,
    prefix_key_cache,
    prefix_owner,
    token_counts,
):
    tensor_index = lax.axis_index("tensor")
    tensor_count = lax.axis_size("tensor")
    seq_count = lax.axis_size("seq")
    length = hidden.shape[0]
    head_size = HEAD_DIM
    whole = lax.all_gather(hidden, "tensor", axis=1, tiled=True)
    wide = whole.astype(jnp.float32)
    normalized_input = (
        wide
        * lax.rsqrt(jnp.mean(wide * wide, axis=1, keepdims=True) + eps)
        * norm_gain.astype(jnp.float32)
    ).astype(jnp.bfloat16)
    width_query = w_query.shape[1]
    full_width = key_value_weight.shape[1]
    heads_dev = width_query // head_size
    kv_heads = full_width // (2 * head_size)

    def contract(piece):
        return jnp.dot(normalized_input, piece, preferred_element_type=jnp.float32)

    query_vectors = contract(lax.all_gather(w_query, "seq", axis=0, tiled=True))
    key_value_pair = contract(lax.all_gather(key_value_weight, "seq", axis=0, tiled=True))
    counts = token_counts[0]
    num_groups = counts.shape[0]
    starts, prefix_group, offset = layout(counts, length)
    positions = PREFIX_LENGTH + offset
    query_vectors = rotate(query_vectors.reshape(length, heads_dev, head_size), positions).astype(
        jnp.bfloat16
    )
    pair_blocks = key_value_pair.reshape(length, kv_heads, 2, head_size)
    rotated_keys = rotate(pair_blocks[:, :, 0], positions)
    pair_all = jnp.stack([rotated_keys, pair_blocks[:, :, 1]], axis=2).astype(jnp.bfloat16)
    suffix_full = pair_all.reshape(length, full_width)
    share = full_width // tensor_count
    suffix_part = lax.dynamic_slice_in_dim(suffix_full, tensor_index * share, share, 1)
    group_full = heads_dev * tensor_count // kv_heads
    kv_local = max(1, heads_dev // group_full)
    kv_start = tensor_index * heads_dev // group_full
    suffix_mine = lax.dynamic_slice_in_dim(pair_all, kv_start, kv_local, 1)
    suffix_keys = suffix_mine[:, :, 0]
    suffix_values = suffix_mine[:, :, 1]
    cache_all = prefix_key_cache[0].reshape(-1, kv_heads, 2, head_size)
    cache_mine = lax.dynamic_slice_in_dim(cache_all, kv_start, kv_local, 1)
    cache_keys = cache_mine[:, :, 0]
    cache_values = cache_mine[:, :, 1]
    group_width = heads_dev // kv_local
    capacity = 2 * length // seq_count
    labels = jnp.arange(num_groups, dtype=jnp.int32)
    owner_match = prefix_owner[None, :] == jnp.arange(seq_count, dtype=jnp.int32)[:, None]
    owner_start = jnp.sum(jnp.where(owner_match, starts[None, :], 0), axis=1)
    owner_count = jnp.sum(jnp.where(owner_match, counts[None, :], 0), axis=1)
    slots = jnp.arange(capacity, dtype=jnp.int32)
    valid = slots[None, :] < owner_count[:, None]
    source_rows = jnp.where(valid, owner_start[:, None] + slots[None, :], 0)
    flat_query = query_vectors.reshape(length, width_query)
    outgoing = jnp.where(valid[:, :, None], flat_query[source_rows], jnp.zeros((), jnp.bfloat16))
    arrived = lax.all_to_all(outgoing, "seq", split_axis=0, concat_axis=0, tiled=True)
    items = arrived.shape[1]
    rows_in = arrived.reshape(seq_count * items, heads_dev, head_size)
    outs = []
    logs = []
    for serve_head in range(heads_dev):
        serve_result, serve_logsum = attend(
            rows_in[:, serve_head],
            cache_keys[:, serve_head // group_width],
            cache_values[:, serve_head // group_width],
            None,
        )
        outs.append(serve_result)
        logs.append(serve_logsum)
    out_block = jnp.stack(outs, axis=1).astype(jnp.bfloat16).reshape(seq_count, items, width_query)
    log_block = jnp.stack(logs, axis=1).reshape(seq_count, items, heads_dev)
    prefix_out = lax.all_to_all(out_block, "seq", split_axis=0, concat_axis=0, tiled=True)
    prefix_log = lax.all_to_all(
        log_block.astype(jnp.bfloat16), "seq", split_axis=0, concat_axis=0, tiled=True
    ).astype(log_block.dtype)
    owner_of_token = jnp.sum(
        jnp.where(prefix_group[:, None] == labels[None, :], prefix_owner[None, :], 0), axis=1
    )
    back_rows = owner_of_token * capacity + offset
    prefix_rows = prefix_out.reshape(seq_count * capacity, heads_dev, head_size)[back_rows]
    prefix_logsum = prefix_log.reshape(seq_count * capacity, heads_dev)[back_rows]
    places = jnp.arange(length, dtype=jnp.int32)
    allowed = (prefix_group[:, None] == prefix_group[None, :]) & (
        places[None, :] <= places[:, None]
    )
    outs = []
    logs = []
    for head in range(heads_dev):
        result, logsum = attend(
            query_vectors[:, head],
            suffix_keys[:, head // group_width],
            suffix_values[:, head // group_width],
            allowed,
        )
        outs.append(result)
        logs.append(logsum)
    suffix_attn = jnp.stack(outs, axis=1)
    suffix_logsum = jnp.stack(logs, axis=1)
    upper = jnp.maximum(prefix_logsum, suffix_logsum)
    left = jnp.exp(prefix_logsum - upper)[..., None]
    right = jnp.exp(suffix_logsum - upper)[..., None]
    context = (
        (left * prefix_rows.astype(jnp.float32) + right * suffix_attn) / (left + right)
    ).astype(jnp.bfloat16)
    context = context.reshape(length, width_query)
    partial_out = jnp.dot(
        context,
        lax.all_gather(w_out, "seq", axis=1, tiled=True),
        preferred_element_type=jnp.float32,
    )
    attn_out = lax.psum_scatter(
        partial_out.astype(jnp.bfloat16), "tensor", scatter_dimension=1, tiled=True
    )
    return (attn_out, suffix_part)


def solution(mesh):
    in_specs = (
        P("seq", "tensor"),
        P(),
        P("seq", "tensor"),
        P("seq", None),
        P("tensor", "seq"),
        P("seq", None, None),
        P(),
        P("seq", None),
    )
    out_specs = (P("seq", "tensor"), P("seq", "tensor"))
    return jax.shard_map(shards, mesh=mesh, in_specs=in_specs, out_specs=out_specs, check_vma=False)
```

profile of v0, /device:TPU:8, one launch (start us, length us, event | category | flops | bytes accessed | tf_op | source)
XLA Modules:
  0.0 541.2 jit_solution(3711993992200430537)
XLA Ops:
  7.2 0.7 all-gather.5.cloned.1.call-update
  7.9 0.7 all-gather.7.cloned.1.call-update
  8.7 0.7 all-gather.9.cloned.1.call-update
  9.4 0.5 all-gather.11.cloned.1.call-update
  10.0 0.7 convert_element_type.73
  10.7 0.7 copy.120
  11.6 0.7 fusion.63
  12.4 2.9 copy.123
  15.8 0.6 pad_clamp_fusion
  16.5 1.0 multiply_cosine_fusion
  17.4 28.1 %all-gather.5.cloned.1.call-done = bf16[128,4096]{1,0:T(8,128)(2,1)} async-done(((bf16[128,512]{1,0:T(8,128)(2,1)}), bf16[128,4096]{1,0:T(8,128)(2,1)}) %all-gather.5.cloned.1.call-update) | async-done | bytes 1048592 | tf_op jit(solution)/shard_map/all_gather | solution.py:66
  45.6 1.5 fusion
  47.1 146.7 %all-gather.7.cloned.1.call-done = bf16[4096,512]{1,0:T(8,128)(2,1)} async-done(((bf16[64,512]{1,0:T(8,128)(2,1)}), bf16[4096,512]{1,0:T(8,128)(2,1)}) %all-gather.7.cloned.1.call-update) | async-done | bytes 4194320 | tf_op jit(solution)/shard_map/all_gather | solution.py:81
  193.8 4.0 fusion.17
  197.8 1.0 reshape.549
  198.8 0.9 fusion.69
  199.7 148.7 %all-gather.9.cloned.1.call-done = bf16[4096,1024]{1,0:T(8,128)(2,1)} async-done(((bf16[64,1024]{1,0:T(8,128)(2,1)}), bf16[4096,1024]{1,0:T(8,128)(2,1)}) %all-gather.9.cloned.1.call-update) | async-done | bytes 8388624 | tf_op jit(solution)/shard_map/all_gather | solution.py:82
  348.5 5.5 %fusion.15 = f32[128,1024]{1,0:T(8,128)} fusion(bf16[4096,1024]{1,0:T(8,128)(2,1)} %all-gather.9.cloned.1.call-done, bf16[128,4096]{1,0:T(8,128)(2,1)S(1)} %copy-done, f32[4096]{0:T(1024)S(1)} %convert_element_type.73, f32[128]{0:T(128)S(1)} %add_rsqrt_fusion), kind=kOutput, calls=%fused_computation.46 | convolution fusion | flops 1075838976 | bytes 9978368 | tf_op jit(solution)/shard_map/dot_general | solution.py:79
  354.0 1.5 reshape.555
  356.1 1.1 multiply_subtract_fusion
  357.3 1.2 gather_fusion
  358.5 0.9 broadcast_select_fusion
  359.4 10.4 %all-to-all-start = ((bf16[64,4,512]{2,1,0:T(4,128)(2,1)}), bf16[64,4,512]{2,1,0:T(4,128)(2,1)S(1)}, u32[]{:S(2)}, u32[]{:S(2)}) async-start(bf16[64,4,512]{2,1,0:T(4,128)(2,1)} %broadcast_select_fusion), calls=%async_computation | async-start | bytes 524288 | tf_op jit(solution)/shard_map/all_to_all | solution.py:117
  370.4 0.6 fusion.33
  371.2 0.6 copy-done.35
  371.8 0.6 fusion.32
  372.5 0.6 fusion.31
  373.2 0.8 convolution_bitcast_fusion
  374.0 14.2 %all-to-all-done = bf16[64,4,512]{2,1,0:T(4,128)(2,1)S(1)} async-done(((bf16[64,4,512]{2,1,0:T(4,128)(2,1)}), bf16[64,4,512]{2,1,0:T(4,128)(2,1)S(1)}, u32[]{:S(2)}, u32[]{:S(2)}) %all-to-all-start) | async-done | bytes 262176 | tf_op jit(solution)/shard_map/all_to_all | solution.py:117
  388.3 1.1 fusion.68
  389.4 0.4 fusion.74
  390.3 0.5 copy-done.23
  390.8 0.5 add_convert_fusion
  391.3 0.8 add.239
  392.1 1.3 fusion.75
  393.4 1.0 copy-done.1
  394.7 0.5 copy-done.24
  395.2 0.5 add_convert_fusion.1
  395.7 1.4 add.237
  397.1 1.3 fusion.76
  398.4 1.0 copy-done.3
  399.7 0.6 copy-done.26
  400.3 0.6 add_convert_fusion.2
  400.9 1.4 add.235
  402.6 1.0 copy-done.5
  404.1 0.8 pad_maximum_fusion.1
  404.8 0.7 copy.125
  405.5 5.5 %all-to-all-start.1 = ((bf16[64,4,4]{1,2,0:T(4,128)(2,1)}), bf16[64,4,4]{1,2,0:T(4,128)(2,1)S(1)}, u32[]{:S(2)}, u32[]{:S(2)}) async-start(bf16[64,4,4]{1,2,0:T(4,128)(2,1)} %copy.125), calls=%async_computation.1 | async-start | bytes 131072 | tf_op jit(solution)/shard_map/all_to_all | solution.py:134
  411.1 1.1 fusion.6
  412.3 0.4 fusion.5
  412.7 0.8 copy-done.4
  413.5 0.4 fusion.4
  413.9 0.8 copy-done.6
  414.8 0.4 fusion.3
  415.5 0.8 convert_element_type.83
  416.3 9.3 %all-to-all-done.1 = bf16[64,4,4]{1,2,0:T(4,128)(2,1)S(1)} async-done(((bf16[64,4,4]{1,2,0:T(4,128)(2,1)}), bf16[64,4,4]{1,2,0:T(4,128)(2,1)S(1)}, u32[]{:S(2)}, u32[]{:S(2)}) %all-to-all-start.1) | async-done | bytes 2080 | tf_op jit(solution)/shard_map/all_to_all | solution.py:134
  425.6 5.9 %all-to-all-start.2 = ((bf16[64,4,512]{2,1,0:T(4,128)(2,1)}), bf16[64,4,512]{2,1,0:T(4,128)(2,1)S(1)}, u32[]{:S(2)}, u32[]{:S(2)}) async-start(bf16[64,4,512]{2,1,0:T(4,128)(2,1)} %convert_element_type.83), calls=%async_computation.2 | async-start | bytes 524288 | tf_op jit(solution)/shard_map/all_to_all | solution.py:133
  432.6 0.8 gather_fusion.1
  433.5 16.1 %all-to-all-done.2 = bf16[64,4,512]{2,1,0:T(4,128)(2,1)S(1)} async-done(((bf16[64,4,512]{2,1,0:T(4,128)(2,1)}), bf16[64,4,512]{2,1,0:T(4,128)(2,1)S(1)}, u32[]{:S(2)}, u32[]{:S(2)}) %all-to-all-start.2) | async-done | bytes 262176 | tf_op jit(solution)/shard_map/all_to_all | solution.py:133
  449.7 0.9 gather_fusion.2
  450.8 44.6 %all-gather.11.cloned.1.call-done = bf16[512,4096]{0,1:T(8,128)(2,1)} async-done(((bf16[512,64]{0,1:T(8,128)(2,1)}), bf16[512,4096]{0,1:T(8,128)(2,1)}) %all-gather.11.cloned.1.call-update) | async-done | bytes 4194320 | tf_op jit(solution)/shard_map/all_gather | solution.py:169
  495.3 4.7 convolution_convert_fusion
  500.2 0.7 copy.137
  500.9 33.8 %reduce-scatter.2.cloned.1.call-done = bf16[128,512]{1,0:T(8,128)(2,1)} async-done(((bf16[128,4096]{1,0:T(8,128)(2,1)}), bf16[128,512]{1,0:T(8,128)(2,1)}) %reduce-scatter.2.cloned.1.call-update) | async-done | bytes 131088 | tf_op jit(solution)/shard_map/reduce_scatter | solution.py:172
  (134 shorter events, 6.6 us)
Async XLA Ops:
  7.2 38.4 %all-gather.5.cloned.1.call-start = ((), (), s32[]{:S(2)}) async-start(), calls=%async_computation.4 | async-start | bytes 1179648 | tf_op jit(solution)/shard_map/all_gather | solution.py:66
  7.9 185.9 %all-gather.7.cloned.1.call-start = ((), (), s32[]{:S(2)}) async-start(), calls=%async_computation.5 | async-start | bytes 4259840 | tf_op jit(solution)/shard_map/all_gather | solution.py:81
  8.6 339.8 %all-gather.9.cloned.1.call-start = ((), (), s32[]{:S(2)}) async-start(), calls=%async_computation.6 | async-start | bytes 8519680 | tf_op jit(solution)/shard_map/all_gather | solution.py:82
  9.4 486.0 %all-gather.11.cloned.1.call-start = ((), (), s32[]{:S(2)}) async-start(), calls=%async_computation.7 | async-start | bytes 4259840 | tf_op jit(solution)/shard_map/all_gather | solution.py:169
  12.4 2.9 copy-start.28
  12.4 2.9 copy-start.42
  47.1 301.4 %copy-start = (bf16[128,4096]{1,0:T(8,128)(2,1)S(1)}, bf16[128,4096]{1,0:T(8,128)(2,1)}, u32[]{:S(2)}) copy-start(bf16[128,4096]{1,0:T(8,128)(2,1)} %all-gather.5.cloned.1.call-done) | copy-start | bytes 3145732
  354.0 2.1 copy-start.7
  354.0 2.1 copy-start.8
  359.4 28.7 %all-to-all-start = ((bf16[64,4,512]{2,1,0:T(4,128)(2,1)}), bf16[64,4,512]{2,1,0:T(4,128)(2,1)S(1)}, u32[]{:S(2)}, u32[]{:S(2)}) async-start(bf16[64,4,512]{2,1,0:T(4,128)(2,1)} %broadcast_select_fusion), calls=%async_computation | async-start | bytes 524288 | tf_op jit(solution)/shard_map/all_to_all | solution.py:117
  370.1 3.9 copy-start.29
  370.3 0.9 copy-start.31
  370.3 19.0 %copy-start.9 = (f32[128,128]{0,1:T(8,128)}, f32[128,128]{0,1:T(8,128)S(1)}, u32[]{:S(2)}) copy-start(f32[128,128]{0,1:T(8,128)S(1)} %get-tuple-element.36) | copy-start | bytes 196612
  370.4 3.6 copy-start.33
  371.2 0.6 copy-start.35
  371.2 18.2 %copy-start.11 = (f32[128,128]{0,1:T(8,128)}, f32[128,128]{0,1:T(8,128)S(1)}, u32[]{:S(2)}) copy-start(f32[128,128]{0,1:T(8,128)S(1)} %get-tuple-element.38) | copy-start | bytes 196612
  372.5 1.5 copy-start.13
  372.5 1.5 copy-start.39
  389.7 0.5 copy-start.16
  390.3 0.5 copy-start.23
  393.4 1.0 copy-start.1
  393.4 1.3 copy-start.17
  394.6 0.5 copy-start.24
  398.3 1.0 copy-start.3
  398.3 1.3 copy-start.19
  399.7 0.6 copy-start.26
  402.6 1.0 copy-start.5
  402.6 1.3 copy-start.21
  405.5 20.1 %all-to-all-start.1 = ((bf16[64,4,4]{1,2,0:T(4,128)(2,1)}), bf16[64,4,4]{1,2,0:T(4,128)(2,1)S(1)}, u32[]{:S(2)}, u32[]{:S(2)}) async-start(bf16[64,4,4]{1,2,0:T(4,128)(2,1)} %copy.125), calls=%async_computation.1 | async-start | bytes 131072 | tf_op jit(solution)/shard_map/all_to_all | solution.py:134
  411.1 1.2 copy-start.2
  411.1 1.2 copy-start.18
  411.1 1.2 copy-start.25
  412.3 1.2 copy-start.4
  412.3 1.2 copy-start.20
  412.3 1.2 copy-start.27
  413.5 1.2 copy-start.6
  413.5 1.2 copy-start.22
  415.1 16.4 %copy-start.10 = (f32[128,128]{0,1:T(8,128)S(1)}, f32[128,128]{0,1:T(8,128)}, u32[]{:S(2)}) copy-start(f32[128,128]{0,1:T(8,128)} %copy-done.9) | copy-start | bytes 196612
  415.2 16.4 %copy-start.32 = (f32[128]{0:T(128)S(1)}, f32[128]{0:T(128)}, u32[]{:S(2)}) copy-start(f32[128]{0:T(128)} %copy-done.31) | copy-start | bytes 1540
  415.2 16.4 %copy-start.37 = (f32[128]{0:T(128)S(1)}, f32[128]{0:T(128)}, u32[]{:S(2)}) copy-start(f32[128]{0:T(128)} %fusion.33) | copy-start | bytes 1540
  415.2 16.6 %copy-start.12 = (f32[128,128]{0,1:T(8,128)S(1)}, f32[128,128]{0,1:T(8,128)}, u32[]{:S(2)}) copy-start(f32[128,128]{0,1:T(8,128)} %copy-done.11) | copy-start | bytes 196612
  415.2 16.6 %copy-start.36 = (f32[128]{0:T(128)S(1)}, f32[128]{0:T(128)}, u32[]{:S(2)}) copy-start(f32[128]{0:T(128)} %copy-done.35) | copy-start | bytes 1540
  415.2 16.6 %copy-start.38 = (f32[128]{0:T(128)S(1)}, f32[128]{0:T(128)}, u32[]{:S(2)}) copy-start(f32[128]{0:T(128)} %fusion.32) | copy-start | bytes 1540
  415.2 16.8 %copy-start.14 = (f32[128,128]{0,1:T(8,128)S(1)}, f32[128,128]{0,1:T(8,128)}, u32[]{:S(2)}) copy-start(f32[128,128]{0,1:T(8,128)} %copy-done.13) | copy-start | bytes 196612
  415.2 16.8 %copy-start.40 = (f32[128]{0:T(128)S(1)}, f32[128]{0:T(128)}, u32[]{:S(2)}) copy-start(f32[128]{0:T(128)} %copy-done.39) | copy-start | bytes 1540
  415.2 16.8 %copy-start.41 = (f32[128]{0:T(128)S(1)}, f32[128]{0:T(128)}, u32[]{:S(2)}) copy-start(f32[128]{0:T(128)} %fusion.31) | copy-start | bytes 1540
  415.2 17.1 %copy-start.30 = (f32[128]{0:T(128)S(1)}, f32[128]{0:T(128)}, u32[]{:S(2)}) copy-start(f32[128]{0:T(128)} %copy-done.29) | copy-start | bytes 1540
  415.2 17.1 %copy-start.34 = (f32[128]{0:T(128)S(1)}, f32[128]{0:T(128)}, u32[]{:S(2)}) copy-start(f32[128]{0:T(128)} %copy-done.33) | copy-start | bytes 1540
  415.3 35.4 %copy-start.15 = (f32[128,1,128]{0,2,1:T(8,128)S(1)}, f32[128,1,128]{0,2,1:T(8,128)}, u32[]{:S(2)}) copy-start(f32[128,1,128]{0,2,1:T(8,128)} %convolution_bitcast_fusion) | copy-start | bytes 196612
  425.6 24.0 %all-to-all-start.2 = ((bf16[64,4,512]{2,1,0:T(4,128)(2,1)}), bf16[64,4,512]{2,1,0:T(4,128)(2,1)S(1)}, u32[]{:S(2)}, u32[]{:S(2)}) async-start(bf16[64,4,512]{2,1,0:T(4,128)(2,1)} %convert_element_type.83), calls=%async_computation.2 | async-start | bytes 524288 | tf_op jit(solution)/shard_map/all_to_all | solution.py:133
  431.5 103.2 %reduce-scatter.2.cloned.1.call-start = ((), (), s32[]{:S(2)}) async-start(), calls=%async_computation.8 | async-start | bytes 1179648 | tf_op jit(solution)/shard_map/reduce_scatter | solution.py:172
Sparse Core Ops, SparseCore 0:
  10.1 35.3 all-gather.4
  48.5 145.2 all-gather.6
  196.7 151.7 all-gather.8
  351.3 144.0 all-gather.10
  500.1 34.5 reduce-scatter.1
where the time goes:
time: 542 us; the launch traced here: 541 us
  waiting for transfers between devices  444 us (82%)
  local copies, waits for them, and re-layouts  25.9 us (5%)
  starting transfers between devices  22 us (4%)
  matrix products  21.8 us (4%)
  between operations  14.5 us (3%)
  other arithmetic  13 us (2%)
    all_gather x1, waiting for transfers between devices, shards(): lax.all_gather(key_value_weight, 'seq', axis=0, tiled=True)  149 us
    all_gather x1, waiting for transfers between devices, shards(): query_vectors = contract(lax.all_gather(w_query, 'seq', axis=0, tiled=True))  147 us
    all_gather x1, waiting for transfers between devices, shards(): lax.all_gather(w_out, 'seq', axis=1, tiled=True)  44.6 us
    reduce_scatter x1, waiting for transfers between devices, shards(): lax.psum_scatter(partial_out.astype(jnp.bfloat16), 'tensor', scatter_dime...  33.8 us
    all_gather x1, waiting for transfers between devices, shards(): whole = lax.all_gather(hidden, 'tensor', axis=1, tiled=True)  28.1 us
    all_to_all x1, waiting for transfers between devices, shards(): lax.all_to_all(out_block, 'seq', split_axis=0, concat_axis=0, tiled=True)  16.1 us
    all_to_all x1, waiting for transfers between devices, shards(): lax.all_to_all(outgoing, 'seq', split_axis=0, concat_axis=0, tiled=True)  14.2 us
    unnamed x90, local copies, waits for them, and re-layouts  10.9 us
  transfers between devices with their start and end apart: 8, of which 8 were waited for; matrix products, arithmetic and copies ran while one was open for 9% of the time, Pallas kernels for 0%

commit v1 on v0

--- a/solution.py
+++ b/solution.py
@@ -7,6 +7,14 @@
 PREFIX_LENGTH = 1024
 eps = 1e-06
 theta = 5000000.0
+
+
+def _run_zones(x_in, chip_axis):
+    reply = lax.axis_size(chip_axis)
+    carry = jnp.stack(reply * [x_in], 0)
+    frame_out = lax.all_to_all(carry, axis_name=chip_axis, split_axis=0, concat_axis=0)
+    n_now = jnp.concatenate(frame_out, 0)
+    return n_now
 
 
 def rotate(values, positions):
@@ -79,7 +87,7 @@
         return jnp.dot(normalized_input, piece, preferred_element_type=jnp.float32)
 
     query_vectors = contract(lax.all_gather(w_query, "seq", axis=0, tiled=True))
-    key_value_pair = contract(lax.all_gather(key_value_weight, "seq", axis=0, tiled=True))
+    key_value_pair = contract(_run_zones(key_value_weight, "seq"))
     counts = token_counts[0]
     num_groups = counts.shape[0]
     starts, prefix_group, offset = layout(counts, length)

time: 542 us -> 591 us (1.090)
  waiting for transfers between devices: 444 us -> 469 us
  starting transfers between devices: 22 us -> 36.9 us
  local copies, waits for them, and re-layouts: 25.9 us -> 37.9 us
    all_gather x1 -> x0, waiting for transfers between devices: 149 us -> none  [shards(): lax.all_gather(key_value_weight, 'seq', axis=0, tiled=True)]
    all_to_all x0 -> x1, waiting for transfers between devices: none -> 116 us  [_run_zones(): lax.all_to_all(carry, axis_name=chip_axis, split_axis=0, concat_axis=0)]
    all_gather x1, waiting for transfers between devices: 147 us -> 245 us  [shards(): query_vectors = contract(lax.all_gather(w_query, 'seq', axis=0, tiled=True))]
    all_gather x1, waiting for transfers between devices: 44.6 us -> 0.02 us  [shards(): lax.all_gather(w_out, 'seq', axis=1, tiled=True)]
    all_to_all x0 -> x1, starting transfers between devices: none -> 19 us  [_run_zones(): lax.all_to_all(carry, axis_name=chip_axis, split_axis=0, concat_axis=0)]
    dot_general x0 -> x1, local copies, waits for them, and re-layouts: none -> 11.6 us  [contract(): return jnp.dot(normalized_input, piece, preferred_element_type=jnp.float32)]
    all_to_all x1, waiting for transfers between devices: 14.2 us -> 20.1 us  [shards(): lax.all_to_all(outgoing, 'seq', split_axis=0, concat_axis=0, tiled=True)]
  transfers between devices with their start and end apart: 8 -> 8, of which waited for: 8 -> 7; matrix products, arithmetic and copies ran while one was open for 9% -> 9% of each run, Pallas kernels for 0% -> 0%
where the time goes in v1:
time: 591 us; the launch traced here: 590 us
  waiting for transfers between devices  469 us (79%)
  local copies, waits for them, and re-layouts  37.9 us (6%)
  starting transfers between devices  36.9 us (6%)
  matrix products  22.5 us (4%)
  between operations  14.5 us (2%)
  other arithmetic  9.61 us (2%)
    all_gather x1, waiting for transfers between devices, shards(): query_vectors = contract(lax.all_gather(w_query, 'seq', axis=0, tiled=True))  245 us
    all_to_all x1, waiting for transfers between devices, _run_zones(): lax.all_to_all(carry, axis_name=chip_axis, split_axis=0, concat_axis=0)  116 us
    reduce_scatter x1, waiting for transfers between devices, shards(): lax.psum_scatter(partial_out.astype(jnp.bfloat16), 'tensor', scatter_dime...  30.4 us
    all_gather x1, waiting for transfers between devices, shards(): whole = lax.all_gather(hidden, 'tensor', axis=1, tiled=True)  27.8 us
    all_to_all x1, waiting for transfers between devices, shards(): lax.all_to_all(outgoing, 'seq', split_axis=0, concat_axis=0, tiled=True)  20.1 us
    all_to_all x1, starting transfers between devices, _run_zones(): lax.all_to_all(carry, axis_name=chip_axis, split_axis=0, concat_axis=0)  19 us
    all_to_all x1, waiting for transfers between devices, shards(): lax.all_to_all(out_block, 'seq', split_axis=0, concat_axis=0, tiled=True)  18.9 us
  transfers between devices with their start and end apart: 8, of which 7 were waited for; matrix products, arithmetic and copies ran while one was open for 9% of the time, Pallas kernels for 0%

profile of v1, /device:TPU:8, one launch (start us, length us, event | category | flops | bytes accessed | tf_op | source)
XLA Modules:
  0.0 590.4 jit_solution(9682956420404016576)
XLA Ops:
  7.2 5.2 stack.36
  12.4 19.0 %all-to-all-start.2 = ((bf16[64,64,1024]{2,1,0:T(8,128)(2,1)}), bf16[64,64,1024]{2,1,0:T(8,128)(2,1)}, u32[]{:S(2)}, u32[]{:S(2)}) async-start(bf16[64,64,1024]{2,1,0:T(8,128)(2,1)} %stack.36), calls=%async_computation.2 | async-start | bytes 16777216 | tf_op jit(solution)/shard_map/all_to_all | solution.py:15
  31.5 0.7 all-gather.4.cloned.1.call-update
  32.2 0.7 all-gather.6.cloned.1.call-update
  33.0 0.7 all-gather.8.cloned.1.call-update
  34.0 2.9 copy.123
  37.5 0.6 pad_clamp_fusion
  38.3 27.8 %all-gather.4.cloned.1.call-done = bf16[128,4096]{1,0:T(8,128)(2,1)} async-done(((bf16[128,512]{1,0:T(8,128)(2,1)}), bf16[128,4096]{1,0:T(8,128)(2,1)}) %all-gather.4.cloned.1.call-update) | async-done | bytes 1048592 | tf_op jit(solution)/shard_map/all_gather | solution.py:74
  66.2 1.5 fusion
  67.7 245.1 %all-gather.6.cloned.1.call-done = bf16[4096,512]{1,0:T(8,128)(2,1)} async-done(((bf16[64,512]{1,0:T(8,128)(2,1)}), bf16[4096,512]{1,0:T(8,128)(2,1)}) %all-gather.6.cloned.1.call-update) | async-done | bytes 4194320 | tf_op jit(solution)/shard_map/all_gather | solution.py:89
  312.8 4.3 fusion.18
  317.1 115.6 %all-to-all-done.2 = bf16[64,64,1024]{2,1,0:T(8,128)(2,1)} async-done(((bf16[64,64,1024]{2,1,0:T(8,128)(2,1)}), bf16[64,64,1024]{2,1,0:T(8,128)(2,1)}, u32[]{:S(2)}, u32[]{:S(2)}) %all-to-all-start.2) | async-done | bytes 8388640 | tf_op jit(solution)/shard_map/all_to_all | solution.py:15
  432.7 11.6 %copy.129 = bf16[1024,4096]{1,0:T(8,128)(2,1)} copy(bf16[1024,4096]{0,1:T(8,128)(2,1)} %bitcast.14) | data formatting | bytes 16777216 | tf_op jit(solution)/shard_map/dot_general | solution.py:87
  444.3 5.9 %fusion.11 = f32[128,4,2,128]{0,3,2,1:T(8,128)S(1)} fusion(bf16[4,2,128,4096]{3,2,1,0:T(8,128)(2,1)} %bitcast.157, bf16[128,4096]{1,0:T(8,128)(2,1)S(1)} %copy-done.6, f32[4096]{0:T(1024)S(1)} %convert_element_type.73, f32[128]{0:T(128)S(1)} %add_rsqrt_fusion), kind=kOutput, calls=%fused_computation.33 | convolution fusion | flops 1075838976 | bytes 9978368 | tf_op jit(solution)/shard_map/dot_general | solution.py:87
  450.5 1.2 gather_fusion
  451.8 0.9 broadcast_select_fusion
  452.6 5.7 all-to-all-start
  458.4 0.2 fusion.70
  459.0 0.6 fusion.34
  459.9 0.5 copy-done.34
  460.3 0.6 fusion.33
  461.2 0.6 fusion.32
  461.8 0.8 convolution_bitcast_fusion
  462.5 20.1 %all-to-all-done = bf16[64,4,512]{2,1,0:T(4,128)(2,1)S(1)} async-done(((bf16[64,4,512]{2,1,0:T(4,128)(2,1)}), bf16[64,4,512]{2,1,0:T(4,128)(2,1)S(1)}, u32[]{:S(2)}, u32[]{:S(2)}) %all-to-all-start) | async-done | bytes 262176 | tf_op jit(solution)/shard_map/all_to_all | solution.py:125
  482.7 1.1 fusion.69
  483.8 0.4 fusion.74
  484.2 0.3 fusion.16
  484.5 0.3 copy-done.14
  484.8 0.6 copy-done.22
  485.3 0.5 add_convert_fusion
  485.9 0.8 add.239
  486.6 1.3 fusion.75
  487.9 1.0 copy-done
  488.9 0.3 fusion.15
  489.2 0.6 copy-done.23
  489.8 0.5 add_convert_fusion.1
  490.3 1.4 add.237
  491.7 1.3 fusion.76
  492.9 1.0 copy-done.2
  493.9 0.3 fusion.14
  494.3 0.6 copy-done.25
  494.8 0.6 add_convert_fusion.2
  495.4 1.4 add.235
  496.8 0.4 fusion.77
  497.2 1.0 copy-done.4
  498.2 0.3 fusion.13
  498.6 0.8 pad_maximum_fusion.1
  499.4 0.7 copy.125
  500.1 5.8 all-to-all-start.1
  505.9 1.1 fusion.6
  507.2 0.4 fusion.5
  507.5 0.8 copy-done.3
  508.4 0.4 fusion.4
  508.8 0.8 copy-done.5
  509.6 0.4 fusion.3
  510.4 0.8 convert_element_type.83
  511.1 8.9 %all-to-all-done.1 = bf16[64,4,4]{1,2,0:T(4,128)(2,1)S(1)} async-done(((bf16[64,4,4]{1,2,0:T(4,128)(2,1)}), bf16[64,4,4]{1,2,0:T(4,128)(2,1)S(1)}, u32[]{:S(2)}, u32[]{:S(2)}) %all-to-all-start.1) | async-done | bytes 2080 | tf_op jit(solution)/shard_map/all_to_all | solution.py:142
  520.1 6.1 %all-to-all-start.3 = ((bf16[64,4,512]{2,1,0:T(4,128)(2,1)}), bf16[64,4,512]{2,1,0:T(4,128)(2,1)S(1)}, u32[]{:S(2)}, u32[]{:S(2)}) async-start(bf16[64,4,512]{2,1,0:T(4,128)(2,1)} %convert_element_type.83), calls=%async_computation.3 | async-start | bytes 524288 | tf_op jit(solution)/shard_map/all_to_all | solution.py:141
  527.1 0.8 gather_fusion.1
  528.0 18.9 %all-to-all-done.3 = bf16[64,4,512]{2,1,0:T(4,128)(2,1)S(1)} async-done(((bf16[64,4,512]{2,1,0:T(4,128)(2,1)}), bf16[64,4,512]{2,1,0:T(4,128)(2,1)S(1)}, u32[]{:S(2)}, u32[]{:S(2)}) %all-to-all-start.3) | async-done | bytes 262176 | tf_op jit(solution)/shard_map/all_to_all | solution.py:141
  547.0 0.9 gather_fusion.2
  548.1 4.6 convolution_convert_fusion
  552.8 0.7 copy.146
  553.5 30.4 %reduce-scatter.2.cloned.1.call-done = bf16[128,512]{1,0:T(8,128)(2,1)} async-done(((bf16[128,4096]{1,0:T(8,128)(2,1)}), bf16[128,512]{1,0:T(8,128)(2,1)}) %reduce-scatter.2.cloned.1.call-update) | async-done | bytes 131088 | tf_op jit(solution)/shard_map/reduce_scatter | solution.py:180
  (127 shorter events, 4.2 us)
Async XLA Ops:
  12.4 21.3 %copy-start.21 = (bf16[4096]{0:T(1024)(128)(2,1)S(1)}, bf16[4096]{0:T(1024)(128)(2,1)}, u32[]{:S(2)}) copy-start(bf16[4096]{0:T(1024)(128)(2,1)} %param.9) | copy-start | bytes 24580
  12.4 21.3 %copy-start.27 = (s32[1,64]{1,0:T(1,128)S(1)}, s32[1,64]{1,0:T(1,128)}, u32[]{:S(2)}) copy-start(s32[1,64]{1,0:T(1,128)} %param.15) | copy-start | bytes 772
  12.4 420.4 %all-to-all-start.2 = ((bf16[64,64,1024]{2,1,0:T(8,128)(2,1)}), bf16[64,64,1024]{2,1,0:T(8,128)(2,1)}, u32[]{:S(2)}, u32[]{:S(2)}) async-start(bf16[64,64,1024]{2,1,0:T(8,128)(2,1)} %stack.36), calls=%async_computation.2 | async-start | bytes 16777216 | tf_op jit(solution)/shard_map/all_to_all | solution.py:15
  31.4 34.8 %all-gather.4.cloned.1.call-start = ((), (), s32[]{:S(2)}) async-start(), calls=%async_computation.5 | async-start | bytes 1179648 | tf_op jit(solution)/shard_map/all_gather | solution.py:74
  32.2 280.7 %all-gather.6.cloned.1.call-start = ((), (), s32[]{:S(2)}) async-start(), calls=%async_computation.6 | async-start | bytes 4259840 | tf_op jit(solution)/shard_map/all_gather | solution.py:89
  32.9 515.2 %all-gather.8.cloned.1.call-start = ((), (), s32[]{:S(2)}) async-start(), calls=%async_computation.7 | async-start | bytes 4259840 | tf_op jit(solution)/shard_map/all_gather | solution.py:177
  34.0 2.9 copy-start.41
  432.7 11.6 %copy-start.6 = (bf16[128,4096]{1,0:T(8,128)(2,1)S(1)}, bf16[128,4096]{1,0:T(8,128)(2,1)}, u32[]{:S(2)}) copy-start(bf16[128,4096]{1,0:T(8,128)(2,1)} %all-gather.4.cloned.1.call-done) | copy-start | bytes 3145732
  452.6 30.0 %all-to-all-start = ((bf16[64,4,512]{2,1,0:T(4,128)(2,1)}), bf16[64,4,512]{2,1,0:T(4,128)(2,1)S(1)}, u32[]{:S(2)}, u32[]{:S(2)}) async-start(bf16[64,4,512]{2,1,0:T(4,128)(2,1)} %broadcast_select_fusion), calls=%async_computation | async-start | bytes 524288 | tf_op jit(solution)/shard_map/all_to_all | solution.py:125
  458.7 3.8 copy-start.28
  458.9 0.9 copy-start.30
  458.9 24.9 %copy-start.7 = (f32[128,128]{0,1:T(8,128)}, f32[128,128]{0,1:T(8,128)S(1)}, u32[]{:S(2)}) copy-start(f32[128,128]{0,1:T(8,128)S(1)} %get-tuple-element.24) | copy-start | bytes 196612
  459.0 3.5 copy-start.32
  459.8 0.5 copy-start.34
  459.8 24.0 %copy-start.9 = (f32[128,128]{0,1:T(8,128)}, f32[128,128]{0,1:T(8,128)S(1)}, u32[]{:S(2)}) copy-start(f32[128,128]{0,1:T(8,128)S(1)} %get-tuple-element.26) | copy-start | bytes 196612
  461.2 1.4 copy-start.11
  461.2 1.3 copy-start.38
  484.2 0.6 copy-start.14
  484.8 0.6 copy-start.22
  487.9 1.0 copy-start
  487.9 1.3 copy-start.15
  489.2 0.6 copy-start.23
  492.9 1.0 copy-start.2
  492.9 1.3 copy-start.17
  494.3 0.6 copy-start.25
  497.2 1.0 copy-start.4
  497.2 1.3 copy-start.19
  500.1 20.0 %all-to-all-start.1 = ((bf16[64,4,4]{1,2,0:T(4,128)(2,1)}), bf16[64,4,4]{1,2,0:T(4,128)(2,1)S(1)}, u32[]{:S(2)}, u32[]{:S(2)}) async-start(bf16[64,4,4]{1,2,0:T(4,128)(2,1)} %copy.125), calls=%async_computation.1 | async-start | bytes 131072 | tf_op jit(solution)/shard_map/all_to_all | solution.py:142
  505.9 1.2 copy-start.1
  505.9 1.2 copy-start.16
  505.9 1.2 copy-start.24
  507.1 1.2 copy-start.3
  507.1 1.2 copy-start.18
  507.1 1.2 copy-start.26
  508.4 1.2 copy-start.5
  508.4 1.2 copy-start.20
  510.0 16.3 %copy-start.8 = (f32[128,128]{0,1:T(8,128)S(1)}, f32[128,128]{0,1:T(8,128)}, u32[]{:S(2)}) copy-start(f32[128,128]{0,1:T(8,128)} %copy-done.7) | copy-start | bytes 196612
  510.0 16.3 %copy-start.31 = (f32[128]{0:T(128)S(1)}, f32[128]{0:T(128)}, u32[]{:S(2)}) copy-start(f32[128]{0:T(128)} %copy-done.30) | copy-start | bytes 1540
  510.0 16.3 %copy-start.36 = (f32[128]{0:T(128)S(1)}, f32[128]{0:T(128)}, u32[]{:S(2)}) copy-start(f32[128]{0:T(128)} %fusion.34) | copy-start | bytes 1540
  510.0 16.5 %copy-start.10 = (f32[128,128]{0,1:T(8,128)S(1)}, f32[128,128]{0,1:T(8,128)}, u32[]{:S(2)}) copy-start(f32[128,128]{0,1:T(8,128)} %copy-done.9) | copy-start | bytes 196612
  510.0 16.5 %copy-start.35 = (f32[128]{0:T(128)S(1)}, f32[128]{0:T(128)}, u32[]{:S(2)}) copy-start(f32[128]{0:T(128)} %copy-done.34) | copy-start | bytes 1540
  510.0 16.5 %copy-start.37 = (f32[128]{0:T(128)S(1)}, f32[128]{0:T(128)}, u32[]{:S(2)}) copy-start(f32[128]{0:T(128)} %fusion.33) | copy-start | bytes 1540
  510.0 16.6 %copy-start.12 = (f32[128,128]{0,1:T(8,128)S(1)}, f32[128,128]{0,1:T(8,128)}, u32[]{:S(2)}) copy-start(f32[128,128]{0,1:T(8,128)} %copy-done.11) | copy-start | bytes 196612
  510.0 16.6 %copy-start.39 = (f32[128]{0:T(128)S(1)}, f32[128]{0:T(128)}, u32[]{:S(2)}) copy-start(f32[128]{0:T(128)} %copy-done.38) | copy-start | bytes 1540
  510.1 16.6 %copy-start.40 = (f32[128]{0:T(128)S(1)}, f32[128]{0:T(128)}, u32[]{:S(2)}) copy-start(f32[128]{0:T(128)} %fusion.32) | copy-start | bytes 1540
  510.1 16.7 %copy-start.29 = (f32[128]{0:T(128)S(1)}, f32[128]{0:T(128)}, u32[]{:S(2)}) copy-start(f32[128]{0:T(128)} %copy-done.28) | copy-start | bytes 1540
  510.1 16.7 %copy-start.33 = (f32[128]{0:T(128)S(1)}, f32[128]{0:T(128)}, u32[]{:S(2)}) copy-start(f32[128]{0:T(128)} %copy-done.32) | copy-start | bytes 1540
  510.1 37.8 %copy-start.13 = (f32[128,1,128]{0,2,1:T(8,128)S(1)}, f32[128,1,128]{0,2,1:T(8,128)}, u32[]{:S(2)}) copy-start(f32[128,1,128]{0,2,1:T(8,128)} %convolution_bitcast_fusion) | copy-start | bytes 196612
  520.1 26.8 %all-to-all-start.3 = ((bf16[64,4,512]{2,1,0:T(4,128)(2,1)}), bf16[64,4,512]{2,1,0:T(4,128)(2,1)S(1)}, u32[]{:S(2)}, u32[]{:S(2)}) async-start(bf16[64,4,512]{2,1,0:T(4,128)(2,1)} %convert_element_type.83), calls=%async_computation.3 | async-start | bytes 524288 | tf_op jit(solution)/shard_map/all_to_all | solution.py:141
  526.2 57.6 %reduce-scatter.2.cloned.1.call-start = ((), (), s32[]{:S(2)}) async-start(), calls=%async_computation.8 | async-start | bytes 1179648 | tf_op jit(solution)/shard_map/reduce_scatter | solution.py:180
Sparse Core Ops, SparseCore 0:
  34.4 31.7 all-gather.3
  69.1 243.6 all-gather.5
  315.8 188.8 all-gather.7
  552.9 30.9 reduce-scatter.1
